TPU v7x, 32 devices: a whole 2x2x4 slice. The times are simulated.
32 devices in a mesh: row: 4 (over z), col: 8 (over y, x, core).
Axes of the slice: x: 2, y: 2, z: 4, core: 2. Of those that a mesh axis runs over, the one named last changes fastest.
Arguments:
- covariance: float32 [8192, 8192], P('row', 'col'), as said below
- self_block: bfloat16 [8192, 512], P(('row', 'col')), may hold values from -0.25 to 0.25
- wake_block: bfloat16 [16, 4, 128, 128], replicated, may hold values from -0.375 to 0.375
- upstream: int32 [16, 4], replicated, may hold values from -1 to 15, as said below
- process_noise: float32 [8192], P('col'), may hold values from 0.5 to 2
- sensor_turbine: int32 [384], replicated, may hold values from 0 to 15
- azimuth_index: int32 [16], replicated, may hold values from 0 to 71
- sensor_weight: float32 [384, 512], replicated, may hold values from -0.25 to 0.25
- sensor_noise: float32 [384], replicated, may hold values from 0.5 to 2
Outputs:
- posterior: float32 [8192, 8192], P('row', 'col')
- kalman_gain: float32 [8192, 384], P('row', 'col')
Inputs may be any that keep to these rules, and one draw needn't show every extreme that they name: Row t lists distinct turbines other than t that lie upstream of t, valid entries first, then -1; some turbine lists 4. `covariance`: symmetric and positive definite.
All inputs are finite; a program needn't handle non-finite values.
Results may differ from a plain program's by a relative error of at most 0.0048.
Values may be sent and summed in bfloat16 or wider, within the bound.
No kernel may reach another device: no remote copies, remote signals or barrier semaphores. Data moves between devices by JAX's collectives and lax.ppermute only.
A program may use at most 128 MiB of HBM per device.

v0:
```python
import math

import jax
import jax.numpy as jnp
from jax import lax
from jax.sharding import PartitionSpec as P

TURB = 16
SPT = 512
INF = 128
NUP = 4
NAZ = 72


def broadcast(value, axis, root):
    mine = lax.axis_index(axis) == root
    return lax.psum(jnp.where(mine, value, jnp.zeros_like(value)), axis)


def observe_columns(sensor_weight, sensor_turbine, azimuth_index, start, count):
    sensors = sensor_weight.shape[0]
    matches = sensor_turbine[:, None] == jnp.arange(TURB)[None, :]
    rotor_index = jnp.sum(jnp.where(matches, azimuth_index[None, :], 0), axis=1)
    sensor_index = jnp.arange(sensors)
    blade_angle = rotor_index.astype(jnp.float32) * jnp.float32(2.0 * math.pi / NAZ) + (
        sensor_index % 3
    ).astype(jnp.float32) * jnp.float32(2.0 * math.pi / 3.0)
    positions = start + jnp.arange(count)
    turbine_of = positions // SPT
    offset_of = positions % SPT
    widened = jnp.tile(sensor_weight, (1, max(1, count // SPT)))
    weights = lax.dynamic_slice_in_dim(widened, start % SPT, count, 1)
    cosine = jnp.cos(blade_angle)[:, None]
    sine = jnp.sin(blade_angle)[:, None]
    factor = jnp.where(
        offset_of[None, :] < 2 * INF,
        jnp.float32(1.0),
        jnp.where(offset_of[None, :] < 3 * INF, cosine, sine),
    )
    return jnp.where(
        sensor_turbine[:, None] == turbine_of[None, :], weights * factor, jnp.float32(0.0)
    )


def gather_col(local_rows):
    ncol = lax.axis_size("col")
    if ncol > 8:
        return lax.all_gather(local_rows, "col", axis=0, tiled=True)
    pieces = [local_rows]
    for step in range(1, ncol):
        perm = [(c, (c + step) % ncol) for c in range(ncol)]
        pieces.append(lax.ppermute(local_rows, "col", perm))
    stacked = jnp.stack(pieces, 0)
    order = (lax.axis_index("col") - jnp.arange(ncol)) % ncol
    return jnp.take(stacked, order, axis=0).reshape((-1,) + local_rows.shape[1:])


def split_bf16(x):
    high = lax.reduce_precision(x, exponent_bits=8, mantissa_bits=7)
    return high.astype(jnp.bfloat16), (x - high).astype(jnp.bfloat16)


def column_rows(local_rows, col_count):
    nrow = lax.axis_size("row")
    ncol = lax.axis_size("col")
    devices = nrow * ncol
    pieces = []
    for step in range(nrow):
        perm = [(d, ((d % nrow + step) % nrow) * ncol + d // nrow) for d in range(devices)]
        pieces.append(lax.ppermute(local_rows, ("row", "col"), perm))
    stacked = jnp.stack(pieces, 0)
    order = (lax.axis_index("row") - jnp.arange(nrow)) % nrow
    return jnp.take(stacked, order, axis=0).reshape((col_count,) + local_rows.shape[1:])


def coupling_matrix(wake_block, upstream, turbine):
    slots = upstream[turbine]
    blocks = jnp.zeros((INF, TURB, INF), jnp.bfloat16)
    for slot_index in range(NUP):
        anchor = slots[slot_index]
        hit = (jnp.arange(TURB) == anchor)[None, :, None]
        blocks = blocks + jnp.where(
            hit, wake_block[turbine, slot_index][:, None, :], jnp.zeros((), jnp.bfloat16)
        )
    return blocks.reshape(INF, TURB * INF)


def mm(a, b):
    return jnp.dot(a, b, precision=lax.Precision.HIGHEST)


def cholesky_inverse(symmetric):
    size = symmetric.shape[0]
    block = 128 if size % 128 == 0 else size
    count = size // block
    eye = jnp.eye(block, dtype=jnp.float32)
    work = {
        (i, j): symmetric[i * block : (i + 1) * block, j * block : (j + 1) * block]
        for i in range(count)
        for j in range(i + 1)
    }
    lower = {}
    diag_inverse = {}
    for k in range(count):
        lower[k, k] = jnp.linalg.cholesky(work[k, k])
        diag_inverse[k] = jax.scipy.linalg.solve_triangular(lower[k, k], eye, lower=True)
        for i in range(k + 1, count):
            lower[i, k] = mm(work[i, k], diag_inverse[k].T)
        for i in range(k + 1, count):
            for j in range(k + 1, i + 1):
                work[i, j] = work[i, j] - mm(lower[i, k], lower[j, k].T)
    inv = {}
    for i in range(count):
        inv[i, i] = diag_inverse[i]
        for j in range(i - 1, -1, -1):
            total = sum(mm(lower[i, m], inv[m, j]) for m in range(j, i))
            inv[i, j] = -mm(diag_inverse[i], total)
    zero = jnp.zeros((block, block), jnp.float32)
    lower_inverse = jnp.block(
        [[inv[i, j] if j <= i else zero for j in range(count)] for i in range(count)]
    )
    return mm(lower_inverse.T, lower_inverse)


def dot_f32(a, b, dims):
    return lax.dot_general(a, b, (dims, ((), ())), preferred_element_type=jnp.float32)


def shards(
    covariance,
    self_block,
    wake_block,
    upstream,
    process_noise,
    sensor_turbine,
    azimuth_index,
    sensor_weight,
    sensor_noise,
):
    row_count, col_count = covariance.shape
    row_start = lax.axis_index("row") * row_count
    col_start = lax.axis_index("col") * col_count
    per_row = row_count // SPT
    per_col = max(1, col_count // SPT)
    first_turbine = lax.axis_index("row") * per_row

    cov3 = covariance.reshape(per_row, SPT, col_count)
    inflow_part = cov3[:, :INF, :].astype(jnp.bfloat16)
    inflow_all = lax.all_gather(inflow_part, "row", axis=0, tiled=True)
    inflow_all = inflow_all.reshape(TURB * INF, col_count)
    own_rows = gather_col(self_block)
    cov_high, cov_low = split_bf16(cov3)
    blocks = []
    for local in range(per_row):
        turbine = first_turbine + local
        diag_rows = own_rows[local * SPT : (local + 1) * SPT]
        result = dot_f32(diag_rows, cov_high[local], ((1,), (0,))) + dot_f32(
            diag_rows, cov_low[local], ((1,), (0,))
        )
        coupling = coupling_matrix(wake_block, upstream, turbine)
        inflow_sum = dot_f32(coupling, inflow_all, ((1,), (0,)))
        result = jnp.concatenate([result[:INF] + inflow_sum, result[INF:]], 0)
        blocks.append(result.astype(jnp.bfloat16))
    half_product = jnp.concatenate(blocks, 0)

    if col_count >= SPT:
        half3 = half_product.reshape(row_count, per_col, SPT)
        half_inflow = jnp.transpose(half3[:, :, :INF], (1, 0, 2))
        half_inflow_all = lax.all_gather(half_inflow, "col", axis=0, tiled=True)
        turbine_cols = [half3[:, local, :] for local in range(per_col)]
    else:
        full = lax.all_gather(half_product, "col", axis=1, tiled=True)
        half_inflow_all = jnp.transpose(full.reshape(row_count, TURB, SPT)[:, :, :INF], (1, 0, 2))
        turbine_cols = [lax.dynamic_slice_in_dim(full, (col_start // SPT) * SPT, SPT, 1)]
    target_rows = column_rows(self_block, col_count)
    piece_width = min(col_count, SPT)
    pieces = []
    for local in range(per_col):
        turbine = col_start // SPT + local
        diag_rows = target_rows[local * piece_width : (local + 1) * piece_width]
        result = lax.optimization_barrier(dot_f32(turbine_cols[local], diag_rows, ((1,), (1,))))
        coupling = coupling_matrix(wake_block, upstream, turbine).reshape(INF, TURB, INF)
        inflow_sum = dot_f32(half_inflow_all, coupling, ((0, 2), (1, 2)))
        inflow_sum = jnp.where(col_start % SPT == 0, inflow_sum, jnp.float32(0.0))
        pieces.append(jnp.concatenate([result[:, :INF] + inflow_sum, result[:, INF:]], 1))
    predicted = jnp.concatenate(pieces, 1)
    row_ids = row_start + jnp.arange(row_count)
    col_ids = col_start + jnp.arange(col_count)
    predicted = predicted + jnp.where(
        row_ids[:, None] == col_ids[None, :], process_noise[None, :], jnp.float32(0.0)
    )
    predicted = lax.optimization_barrier(predicted)

    col_observe = observe_columns(
        sensor_weight, sensor_turbine, azimuth_index, col_start, col_count
    )
    partial_cross = jnp.dot(predicted, col_observe.T, precision=lax.Precision.HIGH)
    cross_cov = lax.psum(partial_cross, "col")
    row_observe = observe_columns(
        sensor_weight, sensor_turbine, azimuth_index, row_start, row_count
    )
    partial_innovation = jnp.dot(row_observe, cross_cov, precision=lax.Precision.HIGHEST)
    innovation = lax.psum(partial_innovation, "row") + jnp.diag(sensor_noise)
    symmetric = 0.5 * (innovation + innovation.T)
    inverse = cholesky_inverse(symmetric)
    gain_block = jnp.dot(cross_cov, inverse, precision=lax.Precision.HIGH)
    piece = self_block.shape[0]
    own_piece = lax.dynamic_slice_in_dim(cross_cov, lax.axis_index("col") * piece, piece, 0)
    own_piece, innovation = lax.optimization_barrier((own_piece, innovation))
    target_cross = column_rows(own_piece, col_count)
    posterior = predicted - jnp.dot(gain_block, target_cross.T, precision=lax.Precision.HIGH)
    share = gain_block.shape[1] // lax.axis_size("col")
    gain_share = lax.dynamic_slice_in_dim(gain_block, lax.axis_index("col") * share, share, 1)
    return (posterior, gain_share)


def solution(mesh):
    in_specs = (P("row", "col"), P(("row", "col"), None), P(), P(), P("col"), P(), P(), P(), P())
    out_specs = (P("row", "col"), P("row", "col"))
    return jax.shard_map(shards, mesh=mesh, in_specs=in_specs, out_specs=out_specs, check_vma=False)
```

profile of v0, /device:TPU:0, one launch (start us, length us, event | category | flops | bytes accessed | tf_op | source)
XLA Modules:
  0.0 441.6 jit_solution(12988101416279156510)
XLA Ops:
  33.4 8.7 %fusion = (bf16[4,512,1024]{2,1,0:T(8,128)(2,1)}, bf16[4,512,1024]{2,1,0:T(8,128)(2,1)}) fusion(f32[4,512,1024]{2,1,0:T(8,128)} %bitcast.286), kind=kLoop, calls=%fused_computation.5 | loop fusion | flops 8388608 | bytes 16777216 | tf_op jit(solution)/shard_map/convert_element_type | solution.py:60
  73.3 25.1 %all-gather.3.cloned.1.call-done = bf16[16,128,1024]{2,1,0:T(8,128)(2,1)} async-done(((bf16[4,128,1024]{2,1,0:T(8,128)(2,1)}), bf16[16,128,1024]{2,1,0:T(8,128)(2,1)}) %all-gather.3.cloned.1.call-update) | async-done | bytes 4194320 | tf_op jit(solution)/shard_map/all_gather | solution.py:149
  98.4 3.3 fusion.34
  115.1 2.9 collective-permute-start.8
  125.6 3.5 collective-permute-done.8
  141.0 33.6 %all-gather.5.cloned.1.call-done = bf16[16,2048,128]{2,1,0:T(8,128)(2,1)} async-done(((bf16[2,2048,128]{2,1,0:T(8,128)(2,1)}), bf16[16,2048,128]{2,1,0:T(8,128)(2,1)}) %all-gather.5.cloned.1.call-update) | async-done | bytes 8388624 | tf_op jit(solution)/shard_map/all_gather | solution.py:169
  174.5 6.2 %fusion.9 = f32[2048,128]{1,0:T(8,128)S(1)} fusion(bf16[16,2048,128]{2,1,0:T(8,128)(2,1)} %all-gather.5.cloned.1.call-done, f32[2048,512]{1,0:T(8,128)} %copy-done.3, pred[16]{0:T(512)(128)(4,1)S(1)} %iota_compare_fusion.7, pred[16]{0:T(512)(128)(4,1)S(1)} %iota_compare_fusion.8, pred[16]{0:T(512)(128)(4,1)S(1)} %iota_compare_fusion.9, ...), kind=kOutput, calls=%fused_computation.18 | convolution fusion | flops 1076101120 | bytes 10616897 | tf_op jit(solution)/shard_map/dot_general | solution.py:126
  186.7 3.4 copy-done
  190.1 8.7 %fusion.18 = f32[2048,384]{1,0:T(8,128)} fusion(f32[2048,1024]{1,0:T(8,128)S(1)} %maximum_add_fusion, f32[384,1024]{1,0:T(8,128)S(1)} %bitcast.288, f32[384]{0:T(512)S(1)} %get-tuple-element.39, f32[384]{0:T(512)S(1)} %get-tuple-element.38, s32[1024]{0:T(1024)S(1)} %add_select_fusion.3, s32[384]{0:T(512)S(1)} %copy-done.26, ...), kind=kOutput, calls=%fused_computation.41 | convolution fusion | flops 4833804288 | bytes 13117952 | tf_op jit(solution)/shard_map/dot_general | solution.py:197
  201.9 66.5 %all-reduce.3.cloned.1.call-done = f32[2048,384]{1,0:T(8,128)} async-done(((f32[2048,384]{1,0:T(8,128)}), f32[2048,384]{1,0:T(8,128)}) %all-reduce.3.cloned.1.call-update) | async-done | bytes 3145744 | tf_op jit(solution)/shard_map/psum | solution.py:198
  268.4 8.3 %fusion.1 = f32[384,384]{1,0:T(8,128)} fusion(f32[2048,384]{1,0:T(8,128)} %all-reduce.3.cloned.1.call-done, f32[384,2048]{1,0:T(8,128)S(1)} %bitcast.297, f32[384]{0:T(512)S(1)} %get-tuple-element.39, f32[384]{0:T(512)S(1)} %get-tuple-element.38, s32[2048]{0:T(1024)S(1)} %add_select_fusion.1, s32[384]{0:T(512)S(1)} %copy-done.26, ...), kind=kOutput, calls=%fused_computation.8 | convolution fusion | flops 3627810816 | bytes 6898176 | tf_op jit(solution)/shard_map/dot_general | solution.py:202
  278.6 37.6 %all-reduce.5.cloned.1.call-done = f32[384,384]{1,0:T(8,128)} async-done(((f32[384,384]{1,0:T(8,128)}), f32[384,384]{1,0:T(8,128)}) %all-reduce.5.cloned.1.call-update) | async-done | bytes 589840 | tf_op jit(solution)/shard_map/psum | solution.py:203
  318.9 11.7 %cholesky.59 = f32[128,128]{1,0:T(8,128)S(1)} custom-call(f32[128,128]{1,0:T(8,128)S(1)} %fusion.180), custom_call_target="Cholesky" | custom-call | tf_op jit(solution)/shard_map/jit(cholesky)/cholesky | solution.py:105
  332.0 10.2 %custom-call.7 = f32[1,128,128]{1,2,0:T(8,128)S(1)} custom-call(f32[1,128,128]{2,1,0:T(8,128)S(1)} %fusion.168), custom_call_target="InvertDiagBlocksLowerTriangular" | custom-call | tf_op jit(solution)/shard_map/jit(_solve_triangular)/triangular_solve | solution.py:106
  344.4 4.0 collective-permute-start.14
  349.9 3.3 collective-permute-start.12
  353.2 4.5 %collective-permute-start.11 = (f32[256,384]{1,0:T(8,128)}, f32[256,384]{1,0:T(8,128)}, u32[]{:S(2)}, u32[]{:S(2)}) collective-permute-start(f32[256,384]{1,0:T(8,128)} %constant_dynamic-slice_fusion), channel_id=1, source_target_pairs={{0,0},{1,8},{2,16},{3,24},{4,1},{5,9},{6,17},{7,25},{8,2},{9,10},{... | collective-permute-start | bytes 1179656 | tf_op jit(solution)/shard_map/ppermute | solution.py:70
  357.8 11.7 %cholesky.70 = f32[128,128]{1,0:T(8,128)S(1)} custom-call(f32[128,128]{1,0:T(8,128)S(1)} %fusion.178), custom_call_target="Cholesky" | custom-call | tf_op jit(solution)/shard_map/jit(cholesky)/cholesky | solution.py:105
  370.9 9.8 %custom-call.8 = f32[1,128,128]{1,2,0:T(8,128)S(1)} custom-call(f32[1,128,128]{2,1,0:T(8,128)S(1)} %fusion.169), custom_call_target="InvertDiagBlocksLowerTriangular" | custom-call | tf_op jit(solution)/shard_map/jit(_solve_triangular)/triangular_solve | solution.py:106
  381.9 11.7 %cholesky.81 = f32[128,128]{1,0:T(8,128)S(1)} custom-call(f32[128,128]{1,0:T(8,128)S(1)} %fusion.176), custom_call_target="Cholesky" | custom-call | tf_op jit(solution)/shard_map/jit(cholesky)/cholesky | solution.py:105
  394.9 10.0 %custom-call.9 = f32[1,128,128]{1,2,0:T(8,128)S(1)} custom-call(f32[1,128,128]{2,1,0:T(8,128)S(1)} %fusion.170), custom_call_target="InvertDiagBlocksLowerTriangular" | custom-call | tf_op jit(solution)/shard_map/jit(_solve_triangular)/triangular_solve | solution.py:106
  407.6 4.6 %fusion.228 = f32[2048,384]{0,1:T(8,128)S(1)} fusion(f32[2048,384]{1,0:T(8,128)} %all-reduce.3.cloned.1.call-done, f32[384,384]{1,0:T(8,128)S(1)} %fusion.47), kind=kOutput, calls=%fused_computation.405 | convolution fusion | flops 1811939328 | bytes 6881280 | tf_op jit(solution)/shard_map/dot_general | solution.py:206
  415.5 3.2 gather_fusion.2
  420.3 14.5 %convolution_subtract_fusion = f32[2048,1024]{1,0:T(8,128)} fusion(f32[2048,1024]{1,0:T(8,128)} %copy-done, f32[2048,384]{0,1:T(8,128)S(1)} %fusion.228, f32[1024,384]{1,0:T(8,128)S(1)} %bitcast_select_fusion), kind=kOutput, calls=%fused_computation.7 | convolution fusion | flops 4833935360 | bytes 21495808 | tf_op jit(solution)/shard_map/dot_general | solution.py:211
  (255 shorter events, 119.5 us)
Async XLA Ops:
  7.2 25.5 %copy-start.16 = (bf16[256,512]{1,0:T(8,128)(2,1)S(1)}, bf16[256,512]{1,0:T(8,128)(2,1)}, u32[]{:S(2)}) copy-start(bf16[256,512]{1,0:T(8,128)(2,1)} %param.13) | copy-start | bytes 786436
  7.2 91.2 %all-gather.3.cloned.1.call-start = ((), (), s32[]{:S(2)}) async-start(), calls=%async_computation | async-start | bytes 5242880 | tf_op jit(solution)/shard_map/all_gather | solution.py:149
  7.2 39.2 %collective-permute-start = (bf16[256,512]{1,0:T(8,128)(2,1)}, bf16[256,512]{1,0:T(8,128)(2,1)S(1)}, u32[]{:S(2)}, u32[]{:S(2)}) collective-permute-start(bf16[256,512]{1,0:T(8,128)(2,1)} %param.13), channel_id=1, source_target_pairs={{0,1},{1,2},{2,3},{3,4},{4,5},{5,6},{6,7},{7,0},{8,9},{9,10},{10,1... | collective-permute-start | bytes 786440 | tf_op jit(solution)/shard_map/ppermute | solution.py:52
  7.7 40.8 %collective-permute-start.1 = (bf16[256,512]{1,0:T(8,128)(2,1)}, bf16[256,512]{1,0:T(8,128)(2,1)S(1)}, u32[]{:S(2)}, u32[]{:S(2)}) collective-permute-start(bf16[256,512]{1,0:T(8,128)(2,1)} %param.13), channel_id=1, source_target_pairs={{0,2},{1,3},{2,4},{3,5},{4,6},{5,7},{6,0},{7,1},{8,10},{9,11},{10,... | collective-permute-start | bytes 786440 | tf_op jit(solution)/shard_map/ppermute | solution.py:52
  10.3 41.2 %collective-permute-start.2 = (bf16[256,512]{1,0:T(8,128)(2,1)}, bf16[256,512]{1,0:T(8,128)(2,1)S(1)}, u32[]{:S(2)}, u32[]{:S(2)}) collective-permute-start(bf16[256,512]{1,0:T(8,128)(2,1)} %param.13), channel_id=1, source_target_pairs={{0,3},{1,4},{2,5},{3,6},{4,7},{5,0},{6,1},{7,2},{8,11},{9,12},{10,... | collective-permute-start | bytes 786440 | tf_op jit(solution)/shard_map/ppermute | solution.py:52
  12.6 39.6 %collective-permute-start.3 = (bf16[256,512]{1,0:T(8,128)(2,1)}, bf16[256,512]{1,0:T(8,128)(2,1)S(1)}, u32[]{:S(2)}, u32[]{:S(2)}) collective-permute-start(bf16[256,512]{1,0:T(8,128)(2,1)} %param.13), channel_id=1, source_target_pairs={{0,4},{1,5},{2,6},{3,7},{4,0},{5,1},{6,2},{7,3},{8,12},{9,13},{10,... | collective-permute-start | bytes 786440 | tf_op jit(solution)/shard_map/ppermute | solution.py:52
  13.2 39.8 %collective-permute-start.4 = (bf16[256,512]{1,0:T(8,128)(2,1)}, bf16[256,512]{1,0:T(8,128)(2,1)S(1)}, u32[]{:S(2)}, u32[]{:S(2)}) collective-permute-start(bf16[256,512]{1,0:T(8,128)(2,1)} %param.13), channel_id=1, source_target_pairs={{0,5},{1,6},{2,7},{3,0},{4,1},{5,2},{6,3},{7,4},{8,13},{9,14},{10,... | collective-permute-start | bytes 786440 | tf_op jit(solution)/shard_map/ppermute | solution.py:52
  16.0 158.5 %all-gather.5.cloned.1.call-start = ((), (), s32[]{:S(2)}) async-start(), calls=%async_computation.1 | async-start | bytes 9437184 | tf_op jit(solution)/shard_map/all_gather | solution.py:169
  46.5 9.0 %collective-permute-start.5 = (bf16[256,512]{1,0:T(8,128)(2,1)S(1)}, bf16[256,512]{1,0:T(8,128)(2,1)S(1)}, u32[]{:S(2)}, u32[]{:S(2)}) collective-permute-start(bf16[256,512]{1,0:T(8,128)(2,1)S(1)} %copy-done.16), channel_id=1, source_target_pairs={{0,6},{1,7},{2,0},{3,1},{4,2},{5,3},{6,4},{7,5},{8,14},{9,15},{10,... | collective-permute-start | bytes 786440 | tf_op jit(solution)/shard_map/ppermute | solution.py:52
  48.5 8.8 %collective-permute-start.6 = (bf16[256,512]{1,0:T(8,128)(2,1)S(1)}, bf16[256,512]{1,0:T(8,128)(2,1)S(1)}, u32[]{:S(2)}, u32[]{:S(2)}) collective-permute-start(bf16[256,512]{1,0:T(8,128)(2,1)S(1)} %copy-done.16), channel_id=1, source_target_pairs={{0,7},{1,0},{2,1},{3,2},{4,3},{5,4},{6,5},{7,6},{8,15},{9,8},{10,9... | collective-permute-start | bytes 786440 | tf_op jit(solution)/shard_map/ppermute | solution.py:52
  107.4 16.4 %copy-start.26 = (s32[384]{0:T(512)S(1)}, s32[384]{0:T(512)}, u32[]{:S(2)}) copy-start(s32[384]{0:T(512)} %param.17) | copy-start | bytes 4612
  107.5 16.4 %copy-start.29 = (s32[16]{0:T(128)S(1)}, s32[16]{0:T(128)}, u32[]{:S(2)}) copy-start(s32[16]{0:T(128)} %param.18) | copy-start | bytes 196
  107.5 17.2 %copy-start.14 = (f32[384,512]{1,0:T(8,128)S(1)}, f32[384,512]{1,0:T(8,128)}, u32[]{:S(2)}) copy-start(f32[384,512]{1,0:T(8,128)} %param.19) | copy-start | bytes 2359300
  110.7 157.6 %all-reduce.3.cloned.1.call-start = ((), (), s32[]{:S(2)}) async-start(), calls=%async_computation.2 | async-start | bytes 6291456 | tf_op jit(solution)/shard_map/psum | solution.py:198
  110.8 14.9 %collective-permute-start.10 = (bf16[256,512]{1,0:T(8,128)(2,1)S(1)}, bf16[256,512]{1,0:T(8,128)(2,1)S(1)}, u32[]{:S(2)}, u32[]{:S(2)}) collective-permute-start(bf16[256,512]{1,0:T(8,128)(2,1)S(1)} %copy-done.16), channel_id=1, source_target_pairs={{0,24},{1,0},{2,8},{3,16},{4,25},{5,1},{6,9},{7,17},{8,26},{9,2},{... | collective-permute-start | bytes 786440 | tf_op jit(solution)/shard_map/ppermute | solution.py:70
  113.3 12.3 %collective-permute-start.9 = (bf16[256,512]{1,0:T(8,128)(2,1)S(1)}, bf16[256,512]{1,0:T(8,128)(2,1)S(1)}, u32[]{:S(2)}, u32[]{:S(2)}) collective-permute-start(bf16[256,512]{1,0:T(8,128)(2,1)S(1)} %copy-done.16), channel_id=1, source_target_pairs={{0,16},{1,24},{2,0},{3,8},{4,17},{5,25},{6,1},{7,9},{8,18},{9,26},... | collective-permute-start | bytes 786440 | tf_op jit(solution)/shard_map/ppermute | solution.py:70
  115.1 14.1 %collective-permute-start.8 = (bf16[256,512]{1,0:T(8,128)(2,1)S(1)}, bf16[256,512]{1,0:T(8,128)(2,1)S(1)}, u32[]{:S(2)}, u32[]{:S(2)}) collective-permute-start(bf16[256,512]{1,0:T(8,128)(2,1)S(1)} %copy-done.16), channel_id=1, source_target_pairs={{0,8},{1,16},{2,24},{3,0},{4,9},{5,17},{6,25},{7,1},{8,10},{9,18},... | collective-permute-start | bytes 786440 | tf_op jit(solution)/shard_map/ppermute | solution.py:70
  117.9 11.3 %collective-permute-start.7 = (bf16[256,512]{1,0:T(8,128)(2,1)S(1)}, bf16[256,512]{1,0:T(8,128)(2,1)S(1)}, u32[]{:S(2)}, u32[]{:S(2)}) collective-permute-start(bf16[256,512]{1,0:T(8,128)(2,1)S(1)} %copy-done.16), channel_id=1, source_target_pairs={{0,0},{1,8},{2,16},{3,24},{4,1},{5,9},{6,17},{7,25},{8,2},{9,10},{... | collective-permute-start | bytes 786440 | tf_op jit(solution)/shard_map/ppermute | solution.py:70
  198.8 117.4 %all-reduce.5.cloned.1.call-start = ((), (), s32[]{:S(2)}) async-start(), calls=%async_computation.3 | async-start | bytes 1179648 | tf_op jit(solution)/shard_map/psum | solution.py:203
  268.4 47.8 %copy-start.27 = (f32[384]{0:T(512)S(1)}, f32[384]{0:T(512)}, u32[]{:S(2)}) copy-start(f32[384]{0:T(512)} %param.20) | copy-start | bytes 4612
  344.4 68.6 %collective-permute-start.14 = (f32[256,384]{1,0:T(8,128)}, f32[256,384]{1,0:T(8,128)S(1)}, u32[]{:S(2)}, u32[]{:S(2)}) collective-permute-start(f32[256,384]{1,0:T(8,128)} %constant_dynamic-slice_fusion), channel_id=1, source_target_pairs={{0,24},{1,0},{2,8},{3,16},{4,25},{5,1},{6,9},{7,17},{8,26},{9,2},{... | collective-permute-start | bytes 1179656 | tf_op jit(solution)/shard_map/ppermute | solution.py:70
  348.4 64.6 %collective-permute-start.13 = (f32[256,384]{1,0:T(8,128)}, f32[256,384]{1,0:T(8,128)}, u32[]{:S(2)}, u32[]{:S(2)}) collective-permute-start(f32[256,384]{1,0:T(8,128)} %constant_dynamic-slice_fusion), channel_id=1, source_target_pairs={{0,16},{1,24},{2,0},{3,8},{4,17},{5,25},{6,1},{7,9},{8,18},{9,26},... | collective-permute-start | bytes 1179656 | tf_op jit(solution)/shard_map/ppermute | solution.py:70
  349.9 63.1 %collective-permute-start.12 = (f32[256,384]{1,0:T(8,128)}, f32[256,384]{1,0:T(8,128)}, u32[]{:S(2)}, u32[]{:S(2)}) collective-permute-start(f32[256,384]{1,0:T(8,128)} %constant_dynamic-slice_fusion), channel_id=1, source_target_pairs={{0,8},{1,16},{2,24},{3,0},{4,9},{5,17},{6,25},{7,1},{8,10},{9,18},... | collective-permute-start | bytes 1179656 | tf_op jit(solution)/shard_map/ppermute | solution.py:70
  353.2 59.8 %collective-permute-start.11 = (f32[256,384]{1,0:T(8,128)}, f32[256,384]{1,0:T(8,128)}, u32[]{:S(2)}, u32[]{:S(2)}) collective-permute-start(f32[256,384]{1,0:T(8,128)} %constant_dynamic-slice_fusion), channel_id=1, source_target_pairs={{0,0},{1,8},{2,16},{3,24},{4,1},{5,9},{6,17},{7,25},{8,2},{9,10},{... | collective-permute-start | bytes 1179656 | tf_op jit(solution)/shard_map/ppermute | solution.py:70
  (39 other events, 117.2 us)
Sparse Core Ops, SparseCore 0:
  16.1 82.1 all-gather.2
  110.8 63.6 all-gather.4
  198.9 69.4 all-reduce.2
  276.8 39.3 all-reduce.4
where the time goes:
time: 450 us; the launch traced here: 442 us
  waiting for transfers between devices  169 us (38%)
  other arithmetic  111 us (25%)
  matrix products  66.9 us (15%)
  local copies, waits for them, and re-layouts  48.5 us (11%)
  starting transfers between devices  31 us (7%)
  between operations  15.2 us (3%)
    psum x1, waiting for transfers between devices, shards(): cross_cov = lax.psum(partial_cross, 'col')  66.5 us
    psum x1, waiting for transfers between devices, shards(): innovation = lax.psum(partial_innovation, 'row') + jnp.diag(sensor_noise)  37.6 us
    another operation x9, other arithmetic, cholesky_inverse(): lower[k, k] = jnp.linalg.cholesky(work[k, k])  37.2 us
    all_gather x1, waiting for transfers between devices, shards(): half_inflow_all = lax.all_gather(half_inflow, 'col', axis=0, tiled=True)  33.6 us
    another operation x6, other arithmetic, cholesky_inverse(): jax.scipy.linalg.solve_triangular(lower[k, k], eye, lower=True)  31.9 us
    all_gather x1, waiting for transfers between devices, shards(): inflow_all = lax.all_gather(inflow_part, 'row', axis=0, tiled=True)  25.1 us
    dot_general x16, matrix products, dot_f32(): lax.dot_general(a, b, (dims, ((), ())), preferred_element_type=jnp.float32)  24.9 us
    unnamed x100, local copies, waits for them, and re-layouts  24.3 us
  transfers between devices with their start and end apart: 19, of which 7 were waited for; matrix products, arithmetic and copies ran while one was open for 28% of the time, Pallas kernels for 0%

commit v1 on v0

--- a/solution.py
+++ b/solution.py
@@ -53,6 +53,25 @@
     stacked = jnp.stack(pieces, 0)
     order = (lax.axis_index("col") - jnp.arange(ncol)) % ncol
     return jnp.take(stacked, order, axis=0).reshape((-1,) + local_rows.shape[1:])
+
+
+def gather_col_paired(local):
+    ncol = lax.axis_size("col")
+    if ncol % 2 or ncol > 8:
+        return lax.all_gather(local, "col", axis=0, tiled=True)
+    col = lax.axis_index("col")
+    shifts = list(range(0, ncol, 2))
+    mine = [local]
+    for step in shifts[1:]:
+        perm = [(c, (c + step) % ncol) for c in range(ncol)]
+        mine.append(lax.ppermute(local, "col", perm))
+    mine = jnp.stack(mine, 0)
+    theirs = lax.ppermute(mine, "col", [(c, c ^ 1) for c in range(ncol)])
+    stacked = jnp.concatenate([mine, theirs], 0)
+    steps = jnp.asarray(shifts, jnp.int32)
+    sources = jnp.concatenate([(col - steps) % ncol, ((col ^ 1) - steps) % ncol])
+    order = jnp.argsort(sources)
+    return jnp.take(stacked, order, axis=0).reshape((-1,) + local.shape[1:])
 
 
 def split_bf16(x):
@@ -166,7 +185,7 @@
     if col_count >= SPT:
         half3 = half_product.reshape(row_count, per_col, SPT)
         half_inflow = jnp.transpose(half3[:, :, :INF], (1, 0, 2))
-        half_inflow_all = lax.all_gather(half_inflow, "col", axis=0, tiled=True)
+        half_inflow_all = gather_col_paired(half_inflow)
         turbine_cols = [half3[:, local, :] for local in range(per_col)]
     else:
         full = lax.all_gather(half_product, "col", axis=1, tiled=True)
@@ -199,7 +218,7 @@
     row_observe = observe_columns(
         sensor_weight, sensor_turbine, azimuth_index, row_start, row_count
     )
-    partial_innovation = jnp.dot(row_observe, cross_cov, precision=lax.Precision.HIGHEST)
+    partial_innovation = jnp.dot(row_observe, cross_cov, precision=lax.Precision.HIGH)
     innovation = lax.psum(partial_innovation, "row") + jnp.diag(sensor_noise)
     symmetric = 0.5 * (innovation + innovation.T)
     inverse = cholesky_inverse(symmetric)

time: 450 us -> 500 us (1.11)
  other arithmetic: 111 us -> 133 us
  local copies, waits for them, and re-layouts: 48.5 us -> 67.7 us
  waiting for transfers between devices: 169 us -> 176 us
  starting transfers between devices: 31 us -> 37 us
    ppermute x0 -> x4, waiting for transfers between devices: none -> 39.8 us  [the longest x3 39.8 us: gather_col_paired(): mine.append(lax.ppermute(local, 'col', perm))]
    all_gather x1 -> x0, waiting for transfers between devices: 33.6 us -> none  [shards(): half_inflow_all = lax.all_gather(half_inflow, 'col', axis=0, tiled=True)]
    select_n x0 -> x3, other arithmetic: none -> 8.34 us  [the longest x2 7.8 us: gather_col_paired(): return jnp.take(stacked, order, axis=0).reshape((-1,) + local.shape[1:])]
    gather x0 -> x1, local copies, waits for them, and re-layouts: none -> 8.31 us  [gather_col_paired(): return jnp.take(stacked, order, axis=0).reshape((-1,) + local.shape[1:])]
    all_gather x1, waiting for transfers between devices: 25.1 us -> 30.5 us  [shards(): inflow_all = lax.all_gather(inflow_part, 'row', axis=0, tiled=True)]
    unnamed x100 -> x172, local copies, waits for them, and re-layouts: 24.3 us -> 28 us
  transfers between devices with their start and end apart: 19 -> 22, of which waited for: 7 -> 5; matrix products, arithmetic and copies ran while one was open for 28% -> 37% of each run, Pallas kernels for 0% -> 0%
where the time goes in v1:
time: 500 us; the launch traced here: 493 us
  waiting for transfers between devices  176 us (35%)
  other arithmetic  133 us (27%)
  local copies, waits for them, and re-layouts  67.7 us (14%)
  matrix products  64.2 us (13%)
  starting transfers between devices  37 us (7%)
  between operations  15.5 us (3%)
    psum x1, waiting for transfers between devices, shards(): cross_cov = lax.psum(partial_cross, 'col')  67.9 us
    ppermute x3, waiting for transfers between devices, gather_col_paired(): mine.append(lax.ppermute(local, 'col', perm))  39.8 us
    psum x1, waiting for transfers between devices, shards(): innovation = lax.psum(partial_innovation, 'row') + jnp.diag(sensor_noise)  37.6 us
    another operation x9, other arithmetic, cholesky_inverse(): lower[k, k] = jnp.linalg.cholesky(work[k, k])  37.2 us
    another operation x6, other arithmetic, cholesky_inverse(): jax.scipy.linalg.solve_triangular(lower[k, k], eye, lower=True)  31.6 us
    all_gather x1, waiting for transfers between devices, shards(): inflow_all = lax.all_gather(inflow_part, 'row', axis=0, tiled=True)  30.5 us
    unnamed x172, local copies, waits for them, and re-layouts  28 us
    eq x24, other arithmetic, coupling_matrix(): hit = (jnp.arange(TURB) == anchor)[None, :, None]  27.4 us
  transfers between devices with their start and end apart: 22, of which 5 were waited for; matrix products, arithmetic and copies ran while one was open for 37% of the time, Pallas kernels for 0%

profile of v1, /device:TPU:0, one launch (start us, length us, event | category | flops | bytes accessed | tf_op | source)
XLA Modules:
  0.0 493.4 jit_solution(8993387788920343469)
XLA Ops:
  41.2 8.7 %fusion = (bf16[4,512,1024]{2,1,0:T(8,128)(2,1)}, bf16[4,512,1024]{2,1,0:T(8,128)(2,1)}) fusion(f32[4,512,1024]{2,1,0:T(8,128)} %bitcast.299), kind=kLoop, calls=%fused_computation.6 | loop fusion | flops 8388608 | bytes 16777216 | tf_op jit(solution)/shard_map/convert_element_type | solution.py:79
  61.5 4.7 collective-permute-start.8
  84.5 30.5 %all-gather.2.cloned.1.call-done = bf16[16,128,1024]{2,1,0:T(8,128)(2,1)} async-done(((bf16[4,128,1024]{2,1,0:T(8,128)(2,1)}), bf16[16,128,1024]{2,1,0:T(8,128)(2,1)}) %all-gather.2.cloned.1.call-update) | async-done | bytes 4194320 | tf_op jit(solution)/shard_map/all_gather | solution.py:168
  137.3 17.5 %collective-permute-done.11 = bf16[2,2048,128]{2,1,0:T(8,128)(2,1)S(1)} collective-permute-done((bf16[2,2048,128]{2,1,0:T(8,128)(2,1)}, bf16[2,2048,128]{2,1,0:T(8,128)(2,1)S(1)}, u32[]{:S(2)}, u32[]{:S(2)}) %collective-permute-start.11) | collective-permute-done | bytes 1048608 | tf_op jit(solution)/shard_map/ppermute | solution.py:67
  154.7 22.3 %collective-permute-done.12 = bf16[2,2048,128]{2,1,0:T(8,128)(2,1)S(1)} collective-permute-done((bf16[2,2048,128]{2,1,0:T(8,128)(2,1)}, bf16[2,2048,128]{2,1,0:T(8,128)(2,1)S(1)}, u32[]{:S(2)}, u32[]{:S(2)}) %collective-permute-start.12) | collective-permute-done | bytes 1048608 | tf_op jit(solution)/shard_map/ppermute | solution.py:67
  177.1 4.7 collective-permute-start.10
  208.0 4.5 constant_dynamic-update-slice_fusion
  212.5 8.3 %gather_fusion.2 = bf16[8,2,2048,128]{3,2,1,0:T(8,128)(2,1)} fusion(bf16[8,2,2048,128]{3,2,1,0:T(8,128)(2,1)} %constant_dynamic-update-slice_fusion, s32[1024]{0:T(1024)} %pad_clamp_fusion), kind=kCustom, calls=%fused_computation.2 | custom fusion | bytes 16777248 | tf_op jit(solution)/shard_map/jit(_take)/gather | solution.py:74
  220.9 7.8 %bitcast_select_fusion = bf16[16,2048,128]{2,1,0:T(8,128)(2,1)} fusion(bf16[8,2,2048,128]{3,2,1,0:T(8,128)(2,1)} %gather_fusion.2, pred[16]{0:T(512)(128)(4,1)S(1)} %broadcast_in_dim.605), kind=kLoop, calls=%fused_computation.8 | loop fusion | flops 4194304 | bytes 16777232 | tf_op jit(solution)/shard_map/jit(_take)/select_n | solution.py:74
  228.8 6.0 %fusion.10 = f32[2048,128]{1,0:T(8,128)S(1)} fusion(bf16[16,2048,128]{2,1,0:T(8,128)(2,1)} %bitcast_select_fusion, f32[2048,512]{1,0:T(8,128)S(1)} %copy-done.4, pred[16]{0:T(512)(128)(4,1)S(1)} %copy-done.54, pred[16]{0:T(512)(128)(4,1)S(1)} %copy-done.55, pred[16]{0:T(512)(128)(4,1)S(1)} %copy-done.56, pred[16]{0:T(512)(128)(4,1)S(1)} %copy-done.57, ...), kind=kOutput, calls=%fused_computation.22 | convolution fusion | flops 1076101120 | bytes 10616897 | tf_op jit(solution)/shard_map/dot_general | solution.py:145
  244.4 8.7 %fusion.18 = f32[2048,384]{1,0:T(8,128)} fusion(f32[2048,1024]{1,0:T(8,128)S(1)} %maximum_add_fusion, f32[384,1024]{1,0:T(8,128)S(1)} %bitcast.301, f32[384]{0:T(512)S(1)} %get-tuple-element.43, f32[384]{0:T(512)S(1)} %get-tuple-element.42, s32[1024]{0:T(1024)S(1)} %get-tuple-element.80, s32[384]{0:T(512)S(1)} %copy-done.44, ...), kind=kOutput, calls=%fused_computation.44 | convolution fusion | flops 4833804288 | bytes 13117952 | tf_op jit(solution)/shard_map/dot_general | solution.py:216
  256.2 67.9 %all-reduce.3.cloned.1.call-done = f32[2048,384]{1,0:T(8,128)} async-done(((f32[2048,384]{1,0:T(8,128)}), f32[2048,384]{1,0:T(8,128)}) %all-reduce.3.cloned.1.call-update) | async-done | bytes 3145744 | tf_op jit(solution)/shard_map/psum | solution.py:217
  324.2 5.5 %fusion.1 = f32[384,384]{1,0:T(8,128)} fusion(f32[2048,384]{1,0:T(8,128)} %all-reduce.3.cloned.1.call-done, f32[384,2048]{1,0:T(8,128)S(1)} %bitcast.312, f32[384]{0:T(512)S(1)} %copy-done.42, f32[384]{0:T(512)S(1)} %copy-done.40, s32[2048]{0:T(1024)S(1)} %add_select_fusion.1, s32[384]{0:T(512)S(1)} %copy-done.44, ...), kind=kOutput, calls=%fused_computation.11 | convolution fusion | flops 1815871488 | bytes 6898176 | tf_op jit(solution)/shard_map/dot_general | solution.py:221
  331.6 37.6 %all-reduce.5.cloned.1.call-done = f32[384,384]{1,0:T(8,128)} async-done(((f32[384,384]{1,0:T(8,128)}), f32[384,384]{1,0:T(8,128)}) %all-reduce.5.cloned.1.call-update) | async-done | bytes 589840 | tf_op jit(solution)/shard_map/psum | solution.py:222
  372.0 5.1 %collective-permute-start.16 = (f32[256,384]{1,0:T(8,128)}, f32[256,384]{1,0:T(8,128)}, u32[]{:S(2)}, u32[]{:S(2)}) collective-permute-start(f32[256,384]{1,0:T(8,128)} %constant_dynamic-slice_fusion.1), channel_id=1, source_target_pairs={{0,8},{1,16},{2,24},{3,0},{4,9},{5,17},{6,25},{7,1},{8,10},{9,18},... | collective-permute-start | bytes 1179656 | tf_op jit(solution)/shard_map/ppermute | solution.py:89
  378.5 3.9 collective-permute-start.18
  384.0 11.7 %cholesky.59 = f32[128,128]{1,0:T(8,128)S(1)} custom-call(f32[128,128]{1,0:T(8,128)S(1)} %fusion.180), custom_call_target="Cholesky" | custom-call | tf_op jit(solution)/shard_map/jit(cholesky)/cholesky | solution.py:124
  397.1 9.8 %custom-call.7 = f32[1,128,128]{1,2,0:T(8,128)S(1)} custom-call(f32[1,128,128]{2,1,0:T(8,128)S(1)} %fusion.168), custom_call_target="InvertDiagBlocksLowerTriangular" | custom-call | tf_op jit(solution)/shard_map/jit(_solve_triangular)/triangular_solve | solution.py:125
  409.2 11.7 %cholesky.70 = f32[128,128]{1,0:T(8,128)S(1)} custom-call(f32[128,128]{1,0:T(8,128)S(1)} %fusion.178), custom_call_target="Cholesky" | custom-call | tf_op jit(solution)/shard_map/jit(cholesky)/cholesky | solution.py:124
  422.2 10.0 %custom-call.8 = f32[1,128,128]{1,2,0:T(8,128)S(1)} custom-call(f32[1,128,128]{2,1,0:T(8,128)S(1)} %fusion.169), custom_call_target="InvertDiagBlocksLowerTriangular" | custom-call | tf_op jit(solution)/shard_map/jit(_solve_triangular)/triangular_solve | solution.py:125
  433.8 11.7 %cholesky.81 = f32[128,128]{1,0:T(8,128)S(1)} custom-call(f32[128,128]{1,0:T(8,128)S(1)} %fusion.176), custom_call_target="Cholesky" | custom-call | tf_op jit(solution)/shard_map/jit(cholesky)/cholesky | solution.py:124
  446.8 9.8 %custom-call.9 = f32[1,128,128]{1,2,0:T(8,128)S(1)} custom-call(f32[1,128,128]{2,1,0:T(8,128)S(1)} %fusion.170), custom_call_target="InvertDiagBlocksLowerTriangular" | custom-call | tf_op jit(solution)/shard_map/jit(_solve_triangular)/triangular_solve | solution.py:125
  459.0 4.8 fusion.230
  472.1 14.5 %convolution_subtract_fusion = f32[2048,1024]{1,0:T(8,128)} fusion(f32[2048,1024]{1,0:T(8,128)} %copy-done, f32[2048,384]{0,1:T(8,128)S(1)} %fusion.230, f32[1024,384]{1,0:T(8,128)S(1)} %bitcast_select_fusion.1), kind=kOutput, calls=%fused_computation.9 | convolution fusion | flops 4833935360 | bytes 21495808 | tf_op jit(solution)/shard_map/dot_general | solution.py:230
  (344 shorter events, 149.9 us)
Async XLA Ops:
  7.2 107.8 %all-gather.2.cloned.1.call-start = ((), (), s32[]{:S(2)}) async-start(), calls=%async_computation | async-start | bytes 5242880 | tf_op jit(solution)/shard_map/all_gather | solution.py:168
  7.2 47.2 %collective-permute-start = (bf16[256,512]{1,0:T(8,128)(2,1)}, bf16[256,512]{1,0:T(8,128)(2,1)S(1)}, u32[]{:S(2)}, u32[]{:S(2)}) collective-permute-start(bf16[256,512]{1,0:T(8,128)(2,1)} %param.14), channel_id=1, source_target_pairs={{0,1},{1,2},{2,3},{3,4},{4,5},{5,6},{6,7},{7,0},{8,9},{9,10},{10,1... | collective-permute-start | bytes 786440 | tf_op jit(solution)/shard_map/ppermute | solution.py:52
  7.7 48.6 %collective-permute-start.1 = (bf16[256,512]{1,0:T(8,128)(2,1)}, bf16[256,512]{1,0:T(8,128)(2,1)S(1)}, u32[]{:S(2)}, u32[]{:S(2)}) collective-permute-start(bf16[256,512]{1,0:T(8,128)(2,1)} %param.14), channel_id=1, source_target_pairs={{0,2},{1,3},{2,4},{3,5},{4,6},{5,7},{6,0},{7,1},{8,10},{9,11},{10,... | collective-permute-start | bytes 786440 | tf_op jit(solution)/shard_map/ppermute | solution.py:52
  10.3 49.1 %collective-permute-start.2 = (bf16[256,512]{1,0:T(8,128)(2,1)}, bf16[256,512]{1,0:T(8,128)(2,1)S(1)}, u32[]{:S(2)}, u32[]{:S(2)}) collective-permute-start(bf16[256,512]{1,0:T(8,128)(2,1)} %param.14), channel_id=1, source_target_pairs={{0,3},{1,4},{2,5},{3,6},{4,7},{5,0},{6,1},{7,2},{8,11},{9,12},{10,... | collective-permute-start | bytes 786440 | tf_op jit(solution)/shard_map/ppermute | solution.py:52
  12.6 48.9 %collective-permute-start.3 = (bf16[256,512]{1,0:T(8,128)(2,1)}, bf16[256,512]{1,0:T(8,128)(2,1)S(1)}, u32[]{:S(2)}, u32[]{:S(2)}) collective-permute-start(bf16[256,512]{1,0:T(8,128)(2,1)} %param.14), channel_id=1, source_target_pairs={{0,4},{1,5},{2,6},{3,7},{4,0},{5,1},{6,2},{7,3},{8,12},{9,13},{10,... | collective-permute-start | bytes 786440 | tf_op jit(solution)/shard_map/ppermute | solution.py:52
  13.2 53.8 %collective-permute-start.4 = (bf16[256,512]{1,0:T(8,128)(2,1)}, bf16[256,512]{1,0:T(8,128)(2,1)S(1)}, u32[]{:S(2)}, u32[]{:S(2)}) collective-permute-start(bf16[256,512]{1,0:T(8,128)(2,1)} %param.14), channel_id=1, source_target_pairs={{0,5},{1,6},{2,7},{3,0},{4,1},{5,2},{6,3},{7,4},{8,13},{9,14},{10,... | collective-permute-start | bytes 786440 | tf_op jit(solution)/shard_map/ppermute | solution.py:52
  16.0 308.1 %all-reduce.3.cloned.1.call-start = ((), (), s32[]{:S(2)}) async-start(), calls=%async_computation.1 | async-start | bytes 6291456 | tf_op jit(solution)/shard_map/psum | solution.py:217
  54.4 13.3 %collective-permute-start.5 = (bf16[256,512]{1,0:T(8,128)(2,1)S(1)}, bf16[256,512]{1,0:T(8,128)(2,1)S(1)}, u32[]{:S(2)}, u32[]{:S(2)}) collective-permute-start(bf16[256,512]{1,0:T(8,128)(2,1)S(1)} %copy-done.21), channel_id=1, source_target_pairs={{0,6},{1,7},{2,0},{3,1},{4,2},{5,3},{6,4},{7,5},{8,14},{9,15},{10,... | collective-permute-start | bytes 786440 | tf_op jit(solution)/shard_map/ppermute | solution.py:52
  56.4 12.0 %collective-permute-start.6 = (bf16[256,512]{1,0:T(8,128)(2,1)S(1)}, bf16[256,512]{1,0:T(8,128)(2,1)S(1)}, u32[]{:S(2)}, u32[]{:S(2)}) collective-permute-start(bf16[256,512]{1,0:T(8,128)(2,1)S(1)} %copy-done.21), channel_id=1, source_target_pairs={{0,7},{1,0},{2,1},{3,2},{4,3},{5,4},{6,5},{7,6},{8,15},{9,8},{10,9... | collective-permute-start | bytes 786440 | tf_op jit(solution)/shard_map/ppermute | solution.py:52
  59.4 129.5 %collective-permute-start.7 = (bf16[256,512]{1,0:T(8,128)(2,1)S(1)}, bf16[256,512]{1,0:T(8,128)(2,1)}, u32[]{:S(2)}, u32[]{:S(2)}) collective-permute-start(bf16[256,512]{1,0:T(8,128)(2,1)S(1)} %copy-done.21), channel_id=1, source_target_pairs={{0,0},{1,8},{2,16},{3,24},{4,1},{5,9},{6,17},{7,25},{8,2},{9,10},{... | collective-permute-start | bytes 786440 | tf_op jit(solution)/shard_map/ppermute | solution.py:89
  61.5 127.4 %collective-permute-start.8 = (bf16[256,512]{1,0:T(8,128)(2,1)S(1)}, bf16[256,512]{1,0:T(8,128)(2,1)}, u32[]{:S(2)}, u32[]{:S(2)}) collective-permute-start(bf16[256,512]{1,0:T(8,128)(2,1)S(1)} %copy-done.21), channel_id=1, source_target_pairs={{0,8},{1,16},{2,24},{3,0},{4,9},{5,17},{6,25},{7,1},{8,10},{9,18},... | collective-permute-start | bytes 786440 | tf_op jit(solution)/shard_map/ppermute | solution.py:89
  127.6 27.2 %collective-permute-start.11 = (bf16[2,2048,128]{2,1,0:T(8,128)(2,1)}, bf16[2,2048,128]{2,1,0:T(8,128)(2,1)S(1)}, u32[]{:S(2)}, u32[]{:S(2)}) collective-permute-start(bf16[2,2048,128]{2,1,0:T(8,128)(2,1)} %get-tuple-element.11), channel_id=1, source_target_pairs={{0,2},{1,3},{2,4},{3,5},{4,6},{5,7},{6,0},{7,1},{8,10},{9,11},{10,... | collective-permute-start | bytes 3145736 | tf_op jit(solution)/shard_map/ppermute | solution.py:67
  127.6 49.5 %collective-permute-start.12 = (bf16[2,2048,128]{2,1,0:T(8,128)(2,1)}, bf16[2,2048,128]{2,1,0:T(8,128)(2,1)S(1)}, u32[]{:S(2)}, u32[]{:S(2)}) collective-permute-start(bf16[2,2048,128]{2,1,0:T(8,128)(2,1)} %get-tuple-element.11), channel_id=1, source_target_pairs={{0,4},{1,5},{2,6},{3,7},{4,0},{5,1},{6,2},{7,3},{8,12},{9,13},{10,... | collective-permute-start | bytes 3145736 | tf_op jit(solution)/shard_map/ppermute | solution.py:67
  129.0 52.8 %collective-permute-start.13 = (bf16[2,2048,128]{2,1,0:T(8,128)(2,1)}, bf16[2,2048,128]{2,1,0:T(8,128)(2,1)}, u32[]{:S(2)}, u32[]{:S(2)}) collective-permute-start(bf16[2,2048,128]{2,1,0:T(8,128)(2,1)} %get-tuple-element.11), channel_id=1, source_target_pairs={{0,6},{1,7},{2,0},{3,1},{4,2},{5,3},{6,4},{7,5},{8,14},{9,15},{10,... | collective-permute-start | bytes 3145736 | tf_op jit(solution)/shard_map/ppermute | solution.py:67
  154.7 34.2 %collective-permute-start.9 = (bf16[256,512]{1,0:T(8,128)(2,1)S(1)}, bf16[256,512]{1,0:T(8,128)(2,1)}, u32[]{:S(2)}, u32[]{:S(2)}) collective-permute-start(bf16[256,512]{1,0:T(8,128)(2,1)S(1)} %copy-done.21), channel_id=1, source_target_pairs={{0,16},{1,24},{2,0},{3,8},{4,17},{5,25},{6,1},{7,9},{8,18},{9,26},... | collective-permute-start | bytes 786440 | tf_op jit(solution)/shard_map/ppermute | solution.py:89
  177.1 11.9 %collective-permute-start.10 = (bf16[256,512]{1,0:T(8,128)(2,1)S(1)}, bf16[256,512]{1,0:T(8,128)(2,1)}, u32[]{:S(2)}, u32[]{:S(2)}) collective-permute-start(bf16[256,512]{1,0:T(8,128)(2,1)S(1)} %copy-done.21), channel_id=1, source_target_pairs={{0,24},{1,0},{2,8},{3,16},{4,25},{5,1},{6,9},{7,17},{8,26},{9,2},{... | collective-permute-start | bytes 786440 | tf_op jit(solution)/shard_map/ppermute | solution.py:89
  185.2 22.8 %collective-permute-start.14 = (bf16[4,2,2048,128]{3,2,1,0:T(8,128)(2,1)}, bf16[4,2,2048,128]{3,2,1,0:T(8,128)(2,1)}, u32[]{:S(2)}, u32[]{:S(2)}) collective-permute-start(bf16[4,2,2048,128]{3,2,1,0:T(8,128)(2,1)} %pad_maximum_fusion), channel_id=1, source_target_pairs={{0,1},{1,0},{2,3},{3,2},{4,5},{5,4},{6,7},{7,6},{8,9},{9,8},{10,11... | collective-permute-start | bytes 12582920 | tf_op jit(solution)/shard_map/ppermute | solution.py:69
  253.1 116.1 %all-reduce.5.cloned.1.call-start = ((), (), s32[]{:S(2)}) async-start(), calls=%async_computation.2 | async-start | bytes 1179648 | tf_op jit(solution)/shard_map/psum | solution.py:222
  254.7 69.4 %copy-start.40 = (f32[384]{0:T(512)S(1)}, f32[384]{0:T(512)}, u32[]{:S(2)}) copy-start(f32[384]{0:T(512)} %copy-done.39) | copy-start | bytes 4612
  254.8 69.4 %copy-start.42 = (f32[384]{0:T(512)S(1)}, f32[384]{0:T(512)}, u32[]{:S(2)}) copy-start(f32[384]{0:T(512)} %copy-done.41) | copy-start | bytes 4612
  370.4 94.3 %collective-permute-start.15 = (f32[256,384]{1,0:T(8,128)}, f32[256,384]{1,0:T(8,128)S(1)}, u32[]{:S(2)}, u32[]{:S(2)}) collective-permute-start(f32[256,384]{1,0:T(8,128)} %constant_dynamic-slice_fusion.1), channel_id=1, source_target_pairs={{0,0},{1,8},{2,16},{3,24},{4,1},{5,9},{6,17},{7,25},{8,2},{9,10},{... | collective-permute-start | bytes 1179656 | tf_op jit(solution)/shard_map/ppermute | solution.py:89
  372.0 92.6 %collective-permute-start.16 = (f32[256,384]{1,0:T(8,128)}, f32[256,384]{1,0:T(8,128)}, u32[]{:S(2)}, u32[]{:S(2)}) collective-permute-start(f32[256,384]{1,0:T(8,128)} %constant_dynamic-slice_fusion.1), channel_id=1, source_target_pairs={{0,8},{1,16},{2,24},{3,0},{4,9},{5,17},{6,25},{7,1},{8,10},{9,18},... | collective-permute-start | bytes 1179656 | tf_op jit(solution)/shard_map/ppermute | solution.py:89
  377.1 87.5 %collective-permute-start.17 = (f32[256,384]{1,0:T(8,128)}, f32[256,384]{1,0:T(8,128)}, u32[]{:S(2)}, u32[]{:S(2)}) collective-permute-start(f32[256,384]{1,0:T(8,128)} %constant_dynamic-slice_fusion.1), channel_id=1, source_target_pairs={{0,16},{1,24},{2,0},{3,8},{4,17},{5,25},{6,1},{7,9},{8,18},{9,26},... | collective-permute-start | bytes 1179656 | tf_op jit(solution)/shard_map/ppermute | solution.py:89
  378.5 86.1 %collective-permute-start.18 = (f32[256,384]{1,0:T(8,128)}, f32[256,384]{1,0:T(8,128)}, u32[]{:S(2)}, u32[]{:S(2)}) collective-permute-start(f32[256,384]{1,0:T(8,128)} %constant_dynamic-slice_fusion.1), channel_id=1, source_target_pairs={{0,24},{1,0},{2,8},{3,16},{4,25},{5,1},{6,9},{7,17},{8,26},{9,2},{... | collective-permute-start | bytes 1179656 | tf_op jit(solution)/shard_map/ppermute | solution.py:89
  (76 other events, 555.5 us)
Sparse Core Ops, SparseCore 0:
  16.2 98.8 all-gather.1
  253.2 70.8 all-reduce.2
  329.8 39.3 all-reduce.4
